TPU v7x, 512 devices: a whole 4x4x16 slice. The times are simulated.
512 devices in a mesh: blk: 64 (over y, x, z_hi, core), mp: 8 (over z_lo).
Axes of the slice: x: 4, y: 4, z: 16 (z_hi: 2, z_lo: 8; z = z_hi * 8 + z_lo), core: 2. Of those that a mesh axis runs over, the one named last changes fastest.
Arguments:
- queries: bfloat16 [16384, 5120], P('blk', 'mp'), may hold values from -8.5 to 8.5
- suffix_key_rows: bfloat16 [16384, 1024], P('blk', 'mp'), may hold values from -6 to 6
- suffix_value_rows: bfloat16 [16384, 1024], P('blk', 'mp'), may hold values from -6 to 6
- shared_prefix_keys: bfloat16 [2048, 1024], P('blk', 'mp'), may hold values from -8.5 to 8.5
- shared_prefix_values: bfloat16 [2048, 1024], P('blk', 'mp'), may hold values from -6 to 6
- out_weight: bfloat16 [5120, 5120], P('mp', 'blk'), may hold values from -0.078125 to 0.078125
- lengths: int32 [16], replicated, may hold values from 1 to 4096, 16384 in all
Outputs:
- output: bfloat16 [16384, 5120], P('blk', 'mp')
Inputs may be any that keep to these rules, and one draw needn't show every extreme that they name: The lengths sum to 16384; the longest is exactly 4096.
All inputs are finite; a program needn't handle non-finite values.
Results may differ from a plain program's by a relative error of at most 0.019.
Values may be sent and summed in bfloat16 or wider, within the bound.
No kernel may reach another device: no remote copies, remote signals or barrier semaphores. Data moves between devices by JAX's collectives and lax.ppermute only.
A program may use at most 64 MiB of HBM per device.

v0:
```python
import math
import jax
import jax.numpy as jnp
from jax import lax
from jax.sharding import PartitionSpec as P

HEAD_SIZE = 128
MASKED_SCORE = -1e30


def passed_along(block, axis, distance):
    devices = range(lax.axis_size(axis))
    route = [(i - distance, i) for i in devices if i - distance in devices]
    return lax.ppermute(block, axis, route)


def per_device(
    queries,
    suffix_key_rows,
    suffix_value_rows,
    shared_prefix_keys,
    shared_prefix_values,
    out_weight,
    lengths,
):
    tok_rows = queries.shape[0]
    kv_heads = suffix_key_rows.shape[1] // HEAD_SIZE
    q_heads = queries.shape[1] // HEAD_SIZE
    heads_per_group = q_heads // kv_heads
    blocks = lax.axis_size("blk")
    cycle_reach = blocks // 4
    my_block = lax.axis_index("blk")
    score_scale = 1.0 / math.sqrt(HEAD_SIZE)
    heads_of_query = queries.reshape(tok_rows, kv_heads, heads_per_group, HEAD_SIZE)
    req_ends = jnp.cumsum(lengths)
    local_rows = jnp.arange(tok_rows, dtype=jnp.int32)
    query_pos = my_block * tok_rows + local_rows

    def owner_of(position):
        return jnp.sum((position[:, None] >= req_ends[None, :]).astype(jnp.int32), axis=1)

    query_owner = owner_of(query_pos)

    def update(carry_state, key_block, value_block, visible):
        run_max, row_total, accumulated = carry_state
        count = key_block.shape[0]
        key_heads = key_block.reshape(count, kv_heads, HEAD_SIZE)
        value_heads = value_block.reshape(count, kv_heads, HEAD_SIZE)
        scores = (
            jnp.einsum(
                "qhgd,khd->hgqk", heads_of_query, key_heads, preferred_element_type=jnp.float32
            )
            * score_scale
        )
        if visible is not None:
            scores = jnp.where(visible[None, None], scores, MASKED_SCORE)
        new_max = jnp.maximum(run_max, jnp.max(scores, axis=-1))
        weights = jnp.exp(scores - new_max[..., None])
        if visible is not None:
            weights = jnp.where(visible[None, None], weights, 0.0)
        rescale = jnp.exp(run_max - new_max)
        row_total = row_total * rescale + jnp.sum(weights, axis=-1)
        contrib = jnp.einsum(
            "hgqk,khd->hgqd",
            weights.astype(jnp.bfloat16),
            value_heads,
            preferred_element_type=jnp.float32,
        )
        accumulated = accumulated * rescale[..., None] + contrib
        return (new_max, row_total, accumulated)

    start_state = (
        jnp.full((kv_heads, heads_per_group, tok_rows), MASKED_SCORE, jnp.float32),
        jnp.zeros((kv_heads, heads_per_group, tok_rows), jnp.float32),
        jnp.zeros((kv_heads, heads_per_group, tok_rows, HEAD_SIZE), jnp.float32),
    )
    carry_state = update(
        start_state,
        lax.all_gather(shared_prefix_keys, "blk", axis=0, tiled=True),
        lax.all_gather(shared_prefix_values, "blk", axis=0, tiled=True),
        None,
    )

    def visible_from(distance):
        key_pos = (my_block - distance) * tok_rows + local_rows
        key_owner = owner_of(key_pos)
        return (
            (key_owner[None, :] == query_owner[:, None])
            & (key_pos[None, :] <= query_pos[:, None])
            & (key_pos[None, :] >= 0)
        )

    kv_pair = jnp.stack((suffix_key_rows, suffix_value_rows))
    carry_state = update(carry_state, kv_pair[0], kv_pair[1], visible_from(0))

    def advance(distance, loop_carry):
        current, moving = loop_carry
        moving = passed_along(moving, "blk", 1)
        visible = visible_from(distance)
        current = update(current, moving[0], moving[1], visible)
        return (current, moving)

    carry_state, kv_pair = lax.fori_loop(1, cycle_reach + 1, advance, (carry_state, kv_pair))
    run_max, row_total, accumulated = carry_state
    attended = accumulated / row_total[..., None]
    attn = (
        jnp.transpose(attended, (2, 0, 1, 3))
        .reshape(tok_rows, q_heads * HEAD_SIZE)
        .astype(jnp.bfloat16)
    )
    product = jnp.dot(
        attn,
        lax.all_gather(out_weight, "blk", axis=1, tiled=True),
        preferred_element_type=jnp.float32,
    )
    return lax.psum_scatter(product.astype(jnp.bfloat16), "mp", scatter_dimension=1, tiled=True)


def solution(mesh):
    placed = (
        P("blk", "mp"),
        P("blk", "mp"),
        P("blk", "mp"),
        P("blk", "mp"),
        P("blk", "mp"),
        P("mp", "blk"),
        P(),
    )
    return jax.shard_map(
        per_device, mesh=mesh, in_specs=placed, out_specs=P("blk", "mp"), check_vma=False
    )
```

profile of v0, /device:TPU:2, one launch (start us, length us, event | category | flops | bytes accessed | tf_op | source)
XLA Modules:
  0.0 754.1 jit_solution(11717746178946045109)
XLA Ops:
  9.4 192.3 %all_gather.9 = bf16[2048,128]{1,0:T(8,128)(2,1)S(1)} all-gather(bf16[32,128]{1,0:T(8,128)(2,1)} %param.12), channel_id=1, replica_groups=mesh['blk'=64,'mp'=8] {'blk'}, dimensions={0}, use_global_device_ids=true | all-gather | bytes 532480 | tf_op jit(solution)/shard_map/all_gather | solution.py:79
  201.6 148.2 %all_gather.10 = bf16[2048,128]{1,0:T(8,128)(2,1)S(1)} all-gather(bf16[32,128]{1,0:T(8,128)(2,1)S(1)} %copy-done.2), channel_id=1, replica_groups=mesh['blk'=64,'mp'=8] {'blk'}, dimensions={0}, use_global_device_ids=true | all-gather | bytes 532480 | tf_op jit(solution)/shard_map/all_gather | solution.py:80
  354.3 2.3 fusion.29
  357.2 280.1 %while.20 = (s32[]{:T(128)}, f32[1,5,256]{2,1,0:T(8,128)S(1)}, f32[1,5,256]{2,1,0:T(8,128)S(1)}, f32[1,5,256,128]{3,2,1,0:T(8,128)S(1)}, bf16[2,256,128]{2,1,0:T...) while((s32[]{:T(128)}, f32[1,5,256]{2,1,0:T(8,128)S(1)}, ...), condition=%wide.region_10.11_spmd.clone, body=%wide.region_6.0_spmd.clone.sunk | while | flops 171328000 | bytes 6847233 | solution.py:103
  357.2 2.2 collective-permute-start
  359.7 16.6 %collective-permute-done = bf16[2,256,128]{2,1,0:T(8,128)(2,1)S(1)} collective-permute-done((bf16[2,256,128]{2,1,0:T(8,128)(2,1)S(1)}, bf16[2,256,128]{2,1,0:T(8,128)(2,1)S(1)}, u32[]{:S(2)}, u32[]{:S(2)}) %collective-permute-start) | collective-permute-done | bytes 131104 | tf_op jit(solution)/shard_map/while/body/eval_jaxpr/ppermute | solution.py:14
  377.6 1.9 collective-permute-start
  379.8 15.2 %collective-permute-done = bf16[2,256,128]{2,1,0:T(8,128)(2,1)S(1)} collective-permute-done((bf16[2,256,128]{2,1,0:T(8,128)(2,1)S(1)}, bf16[2,256,128]{2,1,0:T(8,128)(2,1)S(1)}, u32[]{:S(2)}, u32[]{:S(2)}) %collective-permute-start) | collective-permute-done | bytes 131104 | tf_op jit(solution)/shard_map/while/body/eval_jaxpr/ppermute | solution.py:14
  396.3 1.9 collective-permute-start
  398.5 14.0 %collective-permute-done = bf16[2,256,128]{2,1,0:T(8,128)(2,1)S(1)} collective-permute-done((bf16[2,256,128]{2,1,0:T(8,128)(2,1)S(1)}, bf16[2,256,128]{2,1,0:T(8,128)(2,1)S(1)}, u32[]{:S(2)}, u32[]{:S(2)}) %collective-permute-start) | collective-permute-done | bytes 131104 | tf_op jit(solution)/shard_map/while/body/eval_jaxpr/ppermute | solution.py:14
  413.8 1.9 collective-permute-start
  416.1 13.7 %collective-permute-done = bf16[2,256,128]{2,1,0:T(8,128)(2,1)S(1)} collective-permute-done((bf16[2,256,128]{2,1,0:T(8,128)(2,1)S(1)}, bf16[2,256,128]{2,1,0:T(8,128)(2,1)S(1)}, u32[]{:S(2)}, u32[]{:S(2)}) %collective-permute-start) | collective-permute-done | bytes 131104 | tf_op jit(solution)/shard_map/while/body/eval_jaxpr/ppermute | solution.py:14
  431.0 1.9 collective-permute-start
  433.2 13.7 %collective-permute-done = bf16[2,256,128]{2,1,0:T(8,128)(2,1)S(1)} collective-permute-done((bf16[2,256,128]{2,1,0:T(8,128)(2,1)S(1)}, bf16[2,256,128]{2,1,0:T(8,128)(2,1)S(1)}, u32[]{:S(2)}, u32[]{:S(2)}) %collective-permute-start) | collective-permute-done | bytes 131104 | tf_op jit(solution)/shard_map/while/body/eval_jaxpr/ppermute | solution.py:14
  448.2 1.9 collective-permute-start
  450.4 13.7 %collective-permute-done = bf16[2,256,128]{2,1,0:T(8,128)(2,1)S(1)} collective-permute-done((bf16[2,256,128]{2,1,0:T(8,128)(2,1)S(1)}, bf16[2,256,128]{2,1,0:T(8,128)(2,1)S(1)}, u32[]{:S(2)}, u32[]{:S(2)}) %collective-permute-start) | collective-permute-done | bytes 131104 | tf_op jit(solution)/shard_map/while/body/eval_jaxpr/ppermute | solution.py:14
  467.6 13.7 %collective-permute-done = bf16[2,256,128]{2,1,0:T(8,128)(2,1)S(1)} collective-permute-done((bf16[2,256,128]{2,1,0:T(8,128)(2,1)S(1)}, bf16[2,256,128]{2,1,0:T(8,128)(2,1)S(1)}, u32[]{:S(2)}, u32[]{:S(2)}) %collective-permute-start) | collective-permute-done | bytes 131104 | tf_op jit(solution)/shard_map/while/body/eval_jaxpr/ppermute | solution.py:14
  484.8 13.7 %collective-permute-done = bf16[2,256,128]{2,1,0:T(8,128)(2,1)S(1)} collective-permute-done((bf16[2,256,128]{2,1,0:T(8,128)(2,1)S(1)}, bf16[2,256,128]{2,1,0:T(8,128)(2,1)S(1)}, u32[]{:S(2)}, u32[]{:S(2)}) %collective-permute-start) | collective-permute-done | bytes 131104 | tf_op jit(solution)/shard_map/while/body/eval_jaxpr/ppermute | solution.py:14
  499.8 1.9 collective-permute-start
  502.0 13.7 %collective-permute-done = bf16[2,256,128]{2,1,0:T(8,128)(2,1)S(1)} collective-permute-done((bf16[2,256,128]{2,1,0:T(8,128)(2,1)S(1)}, bf16[2,256,128]{2,1,0:T(8,128)(2,1)S(1)}, u32[]{:S(2)}, u32[]{:S(2)}) %collective-permute-start) | collective-permute-done | bytes 131104 | tf_op jit(solution)/shard_map/while/body/eval_jaxpr/ppermute | solution.py:14
  519.2 13.7 %collective-permute-done = bf16[2,256,128]{2,1,0:T(8,128)(2,1)S(1)} collective-permute-done((bf16[2,256,128]{2,1,0:T(8,128)(2,1)S(1)}, bf16[2,256,128]{2,1,0:T(8,128)(2,1)S(1)}, u32[]{:S(2)}, u32[]{:S(2)}) %collective-permute-start) | collective-permute-done | bytes 131104 | tf_op jit(solution)/shard_map/while/body/eval_jaxpr/ppermute | solution.py:14
  534.1 1.9 collective-permute-start
  536.4 13.7 %collective-permute-done = bf16[2,256,128]{2,1,0:T(8,128)(2,1)S(1)} collective-permute-done((bf16[2,256,128]{2,1,0:T(8,128)(2,1)S(1)}, bf16[2,256,128]{2,1,0:T(8,128)(2,1)S(1)}, u32[]{:S(2)}, u32[]{:S(2)}) %collective-permute-start) | collective-permute-done | bytes 131104 | tf_op jit(solution)/shard_map/while/body/eval_jaxpr/ppermute | solution.py:14
  553.6 13.7 %collective-permute-done = bf16[2,256,128]{2,1,0:T(8,128)(2,1)S(1)} collective-permute-done((bf16[2,256,128]{2,1,0:T(8,128)(2,1)S(1)}, bf16[2,256,128]{2,1,0:T(8,128)(2,1)S(1)}, u32[]{:S(2)}, u32[]{:S(2)}) %collective-permute-start) | collective-permute-done | bytes 131104 | tf_op jit(solution)/shard_map/while/body/eval_jaxpr/ppermute | solution.py:14
  570.7 13.7 %collective-permute-done = bf16[2,256,128]{2,1,0:T(8,128)(2,1)S(1)} collective-permute-done((bf16[2,256,128]{2,1,0:T(8,128)(2,1)S(1)}, bf16[2,256,128]{2,1,0:T(8,128)(2,1)S(1)}, u32[]{:S(2)}, u32[]{:S(2)}) %collective-permute-start) | collective-permute-done | bytes 131104 | tf_op jit(solution)/shard_map/while/body/eval_jaxpr/ppermute | solution.py:14
  587.9 13.7 %collective-permute-done = bf16[2,256,128]{2,1,0:T(8,128)(2,1)S(1)} collective-permute-done((bf16[2,256,128]{2,1,0:T(8,128)(2,1)S(1)}, bf16[2,256,128]{2,1,0:T(8,128)(2,1)S(1)}, u32[]{:S(2)}, u32[]{:S(2)}) %collective-permute-start) | collective-permute-done | bytes 131104 | tf_op jit(solution)/shard_map/while/body/eval_jaxpr/ppermute | solution.py:14
  605.1 13.7 %collective-permute-done = bf16[2,256,128]{2,1,0:T(8,128)(2,1)S(1)} collective-permute-done((bf16[2,256,128]{2,1,0:T(8,128)(2,1)S(1)}, bf16[2,256,128]{2,1,0:T(8,128)(2,1)S(1)}, u32[]{:S(2)}, u32[]{:S(2)}) %collective-permute-start) | collective-permute-done | bytes 131104 | tf_op jit(solution)/shard_map/while/body/eval_jaxpr/ppermute | solution.py:14
  620.1 1.9 collective-permute-start
  622.3 13.7 %collective-permute-done = bf16[2,256,128]{2,1,0:T(8,128)(2,1)S(1)} collective-permute-done((bf16[2,256,128]{2,1,0:T(8,128)(2,1)S(1)}, bf16[2,256,128]{2,1,0:T(8,128)(2,1)S(1)}, u32[]{:S(2)}, u32[]{:S(2)}) %collective-permute-start) | collective-permute-done | bytes 131104 | tf_op jit(solution)/shard_map/while/body/eval_jaxpr/ppermute | solution.py:14
  637.6 5.1 convolution_convert_fusion
  642.7 2.6 copy.49
  645.3 100.1 %reduce-scatter.4.cloned.1.call-done = bf16[640,256]{1,0:T(8,128)(2,1)} async-done(((bf16[5120,256]{1,0:T(8,128)(2,1)}), bf16[640,256]{1,0:T(8,128)(2,1)}) %reduce-scatter.4.cloned.1.call-update) | async-done | bytes 327696
  (214 shorter events, 47.2 us)
Async XLA Ops:
  6.5 195.1 %copy-start.2 = (bf16[32,128]{1,0:T(8,128)(2,1)S(1)}, bf16[32,128]{1,0:T(8,128)(2,1)}, u32[]{:S(2)}) copy-start(bf16[32,128]{1,0:T(8,128)(2,1)} %param.13) | copy-start | bytes 24580
  6.5 631.1 %all-gather.2.cloned.1.call-start = ((), (), s32[]{:S(2)}) async-start(), calls=%async_computation.1 | async-start | bytes 6656000 | tf_op jit(solution)/shard_map/all_gather | solution.py:113
  7.3 738.1 %reduce-scatter.4.cloned.1.call-start = ((), (), s32[]{:S(2)}) async-start(), calls=%async_computation.2 | async-start | bytes 2949120
  350.4 1.5 copy-start
  354.3 2.4 copy-start.1
  357.2 19.1 %collective-permute-start = (bf16[2,256,128]{2,1,0:T(8,128)(2,1)S(1)}, bf16[2,256,128]{2,1,0:T(8,128)(2,1)S(1)}, u32[]{:S(2)}, u32[]{:S(2)}) collective-permute-start(bf16[2,256,128]{2,1,0:T(8,128)(2,1)S(1)} %get-tuple-element.371), channel_id=1, source_target_pairs={{0,8},{8,16},{16,24},{24,32},{32,40},{40,48},{48,56},{56,64},{64,7... | collective-permute-start | bytes 393224 | tf_op jit(solution)/shard_map/while/body/eval_jaxpr/ppermute | solution.py:14
  377.6 17.4 %collective-permute-start = (bf16[2,256,128]{2,1,0:T(8,128)(2,1)S(1)}, bf16[2,256,128]{2,1,0:T(8,128)(2,1)S(1)}, u32[]{:S(2)}, u32[]{:S(2)}) collective-permute-start(bf16[2,256,128]{2,1,0:T(8,128)(2,1)S(1)} %get-tuple-element.371), channel_id=1, source_target_pairs={{0,8},{8,16},{16,24},{24,32},{32,40},{40,48},{48,56},{56,64},{64,7... | collective-permute-start | bytes 393224 | tf_op jit(solution)/shard_map/while/body/eval_jaxpr/ppermute | solution.py:14
  396.3 16.3 %collective-permute-start = (bf16[2,256,128]{2,1,0:T(8,128)(2,1)S(1)}, bf16[2,256,128]{2,1,0:T(8,128)(2,1)S(1)}, u32[]{:S(2)}, u32[]{:S(2)}) collective-permute-start(bf16[2,256,128]{2,1,0:T(8,128)(2,1)S(1)} %get-tuple-element.371), channel_id=1, source_target_pairs={{0,8},{8,16},{16,24},{24,32},{32,40},{40,48},{48,56},{56,64},{64,7... | collective-permute-start | bytes 393224 | tf_op jit(solution)/shard_map/while/body/eval_jaxpr/ppermute | solution.py:14
  413.8 15.9 %collective-permute-start = (bf16[2,256,128]{2,1,0:T(8,128)(2,1)S(1)}, bf16[2,256,128]{2,1,0:T(8,128)(2,1)S(1)}, u32[]{:S(2)}, u32[]{:S(2)}) collective-permute-start(bf16[2,256,128]{2,1,0:T(8,128)(2,1)S(1)} %get-tuple-element.371), channel_id=1, source_target_pairs={{0,8},{8,16},{16,24},{24,32},{32,40},{40,48},{48,56},{56,64},{64,7... | collective-permute-start | bytes 393224 | tf_op jit(solution)/shard_map/while/body/eval_jaxpr/ppermute | solution.py:14
  431.0 15.9 %collective-permute-start = (bf16[2,256,128]{2,1,0:T(8,128)(2,1)S(1)}, bf16[2,256,128]{2,1,0:T(8,128)(2,1)S(1)}, u32[]{:S(2)}, u32[]{:S(2)}) collective-permute-start(bf16[2,256,128]{2,1,0:T(8,128)(2,1)S(1)} %get-tuple-element.371), channel_id=1, source_target_pairs={{0,8},{8,16},{16,24},{24,32},{32,40},{40,48},{48,56},{56,64},{64,7... | collective-permute-start | bytes 393224 | tf_op jit(solution)/shard_map/while/body/eval_jaxpr/ppermute | solution.py:14
  448.2 15.9 %collective-permute-start = (bf16[2,256,128]{2,1,0:T(8,128)(2,1)S(1)}, bf16[2,256,128]{2,1,0:T(8,128)(2,1)S(1)}, u32[]{:S(2)}, u32[]{:S(2)}) collective-permute-start(bf16[2,256,128]{2,1,0:T(8,128)(2,1)S(1)} %get-tuple-element.371), channel_id=1, source_target_pairs={{0,8},{8,16},{16,24},{24,32},{32,40},{40,48},{48,56},{56,64},{64,7... | collective-permute-start | bytes 393224 | tf_op jit(solution)/shard_map/while/body/eval_jaxpr/ppermute | solution.py:14
  465.4 15.9 %collective-permute-start = (bf16[2,256,128]{2,1,0:T(8,128)(2,1)S(1)}, bf16[2,256,128]{2,1,0:T(8,128)(2,1)S(1)}, u32[]{:S(2)}, u32[]{:S(2)}) collective-permute-start(bf16[2,256,128]{2,1,0:T(8,128)(2,1)S(1)} %get-tuple-element.371), channel_id=1, source_target_pairs={{0,8},{8,16},{16,24},{24,32},{32,40},{40,48},{48,56},{56,64},{64,7... | collective-permute-start | bytes 393224 | tf_op jit(solution)/shard_map/while/body/eval_jaxpr/ppermute | solution.py:14
  482.6 15.9 %collective-permute-start = (bf16[2,256,128]{2,1,0:T(8,128)(2,1)S(1)}, bf16[2,256,128]{2,1,0:T(8,128)(2,1)S(1)}, u32[]{:S(2)}, u32[]{:S(2)}) collective-permute-start(bf16[2,256,128]{2,1,0:T(8,128)(2,1)S(1)} %get-tuple-element.371), channel_id=1, source_target_pairs={{0,8},{8,16},{16,24},{24,32},{32,40},{40,48},{48,56},{56,64},{64,7... | collective-permute-start | bytes 393224 | tf_op jit(solution)/shard_map/while/body/eval_jaxpr/ppermute | solution.py:14
  499.8 15.9 %collective-permute-start = (bf16[2,256,128]{2,1,0:T(8,128)(2,1)S(1)}, bf16[2,256,128]{2,1,0:T(8,128)(2,1)S(1)}, u32[]{:S(2)}, u32[]{:S(2)}) collective-permute-start(bf16[2,256,128]{2,1,0:T(8,128)(2,1)S(1)} %get-tuple-element.371), channel_id=1, source_target_pairs={{0,8},{8,16},{16,24},{24,32},{32,40},{40,48},{48,56},{56,64},{64,7... | collective-permute-start | bytes 393224 | tf_op jit(solution)/shard_map/while/body/eval_jaxpr/ppermute | solution.py:14
  517.0 15.9 %collective-permute-start = (bf16[2,256,128]{2,1,0:T(8,128)(2,1)S(1)}, bf16[2,256,128]{2,1,0:T(8,128)(2,1)S(1)}, u32[]{:S(2)}, u32[]{:S(2)}) collective-permute-start(bf16[2,256,128]{2,1,0:T(8,128)(2,1)S(1)} %get-tuple-element.371), channel_id=1, source_target_pairs={{0,8},{8,16},{16,24},{24,32},{32,40},{40,48},{48,56},{56,64},{64,7... | collective-permute-start | bytes 393224 | tf_op jit(solution)/shard_map/while/body/eval_jaxpr/ppermute | solution.py:14
  534.1 15.9 %collective-permute-start = (bf16[2,256,128]{2,1,0:T(8,128)(2,1)S(1)}, bf16[2,256,128]{2,1,0:T(8,128)(2,1)S(1)}, u32[]{:S(2)}, u32[]{:S(2)}) collective-permute-start(bf16[2,256,128]{2,1,0:T(8,128)(2,1)S(1)} %get-tuple-element.371), channel_id=1, source_target_pairs={{0,8},{8,16},{16,24},{24,32},{32,40},{40,48},{48,56},{56,64},{64,7... | collective-permute-start | bytes 393224 | tf_op jit(solution)/shard_map/while/body/eval_jaxpr/ppermute | solution.py:14
  551.3 15.9 %collective-permute-start = (bf16[2,256,128]{2,1,0:T(8,128)(2,1)S(1)}, bf16[2,256,128]{2,1,0:T(8,128)(2,1)S(1)}, u32[]{:S(2)}, u32[]{:S(2)}) collective-permute-start(bf16[2,256,128]{2,1,0:T(8,128)(2,1)S(1)} %get-tuple-element.371), channel_id=1, source_target_pairs={{0,8},{8,16},{16,24},{24,32},{32,40},{40,48},{48,56},{56,64},{64,7... | collective-permute-start | bytes 393224 | tf_op jit(solution)/shard_map/while/body/eval_jaxpr/ppermute | solution.py:14
  568.5 15.9 %collective-permute-start = (bf16[2,256,128]{2,1,0:T(8,128)(2,1)S(1)}, bf16[2,256,128]{2,1,0:T(8,128)(2,1)S(1)}, u32[]{:S(2)}, u32[]{:S(2)}) collective-permute-start(bf16[2,256,128]{2,1,0:T(8,128)(2,1)S(1)} %get-tuple-element.371), channel_id=1, source_target_pairs={{0,8},{8,16},{16,24},{24,32},{32,40},{40,48},{48,56},{56,64},{64,7... | collective-permute-start | bytes 393224 | tf_op jit(solution)/shard_map/while/body/eval_jaxpr/ppermute | solution.py:14
  585.7 15.9 %collective-permute-start = (bf16[2,256,128]{2,1,0:T(8,128)(2,1)S(1)}, bf16[2,256,128]{2,1,0:T(8,128)(2,1)S(1)}, u32[]{:S(2)}, u32[]{:S(2)}) collective-permute-start(bf16[2,256,128]{2,1,0:T(8,128)(2,1)S(1)} %get-tuple-element.371), channel_id=1, source_target_pairs={{0,8},{8,16},{16,24},{24,32},{32,40},{40,48},{48,56},{56,64},{64,7... | collective-permute-start | bytes 393224 | tf_op jit(solution)/shard_map/while/body/eval_jaxpr/ppermute | solution.py:14
  602.9 15.9 %collective-permute-start = (bf16[2,256,128]{2,1,0:T(8,128)(2,1)S(1)}, bf16[2,256,128]{2,1,0:T(8,128)(2,1)S(1)}, u32[]{:S(2)}, u32[]{:S(2)}) collective-permute-start(bf16[2,256,128]{2,1,0:T(8,128)(2,1)S(1)} %get-tuple-element.371), channel_id=1, source_target_pairs={{0,8},{8,16},{16,24},{24,32},{32,40},{40,48},{48,56},{56,64},{64,7... | collective-permute-start | bytes 393224 | tf_op jit(solution)/shard_map/while/body/eval_jaxpr/ppermute | solution.py:14
  620.1 15.9 %collective-permute-start = (bf16[2,256,128]{2,1,0:T(8,128)(2,1)S(1)}, bf16[2,256,128]{2,1,0:T(8,128)(2,1)S(1)}, u32[]{:S(2)}, u32[]{:S(2)}) collective-permute-start(bf16[2,256,128]{2,1,0:T(8,128)(2,1)S(1)} %get-tuple-element.371), channel_id=1, source_target_pairs={{0,8},{8,16},{16,24},{24,32},{32,40},{40,48},{48,56},{56,64},{64,7... | collective-permute-start | bytes 393224 | tf_op jit(solution)/shard_map/while/body/eval_jaxpr/ppermute | solution.py:14
Sparse Core Ops, SparseCore 0:
  11.8 165.6 all-gather.1
  645.4 99.9 reduce-scatter.3
where the time goes:
time: 756 us; the launch traced here: 754 us
  blocking collectives  341 us (45%)
  waiting for transfers between devices  324 us (43%)
  starting transfers between devices  31.1 us (4%)
  matrix products  25 us (3%)
  between operations  13.6 us (2%)
  other arithmetic  11.1 us (1%)
    ppermute x16, waiting for transfers between devices, passed_along(): return lax.ppermute(block, axis, route)  223 us
    all_gather x1, blocking collectives, per_device(): lax.all_gather(shared_prefix_keys, 'blk', axis=0, tiled=True)  192 us
    all_gather x1, blocking collectives, per_device(): lax.all_gather(shared_prefix_values, 'blk', axis=0, tiled=True)  148 us
    unnamed x3, waiting for transfers between devices  101 us
    ppermute x16, starting transfers between devices, passed_along(): return lax.ppermute(block, axis, route)  31.1 us
  transfers between devices with their start and end apart: 18, of which 17 were waited for; matrix products, arithmetic and copies ran while one was open for 4% of the time, Pallas kernels for 0%

commit v1 on v0

--- a/solution.py
+++ b/solution.py
@@ -76,7 +76,10 @@
     )
     carry_state = update(
         start_state,
-        lax.all_gather(shared_prefix_keys, "blk", axis=0, tiled=True),
+        jnp.concatenate(
+            lax.all_to_all(jnp.stack([shared_prefix_keys] * lax.axis_size("blk")), "blk", 0, 0),
+            axis=0,
+        ),
         lax.all_gather(shared_prefix_values, "blk", axis=0, tiled=True),
         None,
     )

time: 756 us -> 633 us (0.84)
  the two profiles are of different devices: /device:TPU:2 before, /device:TPU:16 now
where the time goes in v1:
time: 633 us; the launch traced here: 631 us
  waiting for transfers between devices  321 us (51%)
  blocking collectives  198 us (31%)
  starting transfers between devices  52.4 us (8%)
  matrix products  25.1 us (4%)
  between operations  13.6 us (2%)
  other arithmetic  11.7 us (2%)
  local copies, waits for them, and re-layouts  7.38 us (1%)
    ppermute x16, waiting for transfers between devices, passed_along(): return lax.ppermute(block, axis, route)  255 us
    all_gather x1, blocking collectives, per_device(): lax.all_gather(shared_prefix_values, 'blk', axis=0, tiled=True)  198 us
    unnamed x3, waiting for transfers between devices  65.8 us
    ppermute x16, starting transfers between devices, passed_along(): return lax.ppermute(block, axis, route)  31 us
    all_to_all x1, starting transfers between devices, per_device(): lax.all_to_all(jnp.stack([shared_prefix_keys] * lax.axis_size('blk')), 'b...  21.3 us
  transfers between devices with their start and end apart: 19, of which 17 were waited for; matrix products, arithmetic and copies ran while one was open for 5% of the time, Pallas kernels for 0%

profile of v1, /device:TPU:16, one launch (start us, length us, event | category | flops | bytes accessed | tf_op | source)
XLA Modules:
  0.0 630.5 jit_solution(6799888633840612891)
XLA Ops:
  8.2 21.3 %all-to-all-start = ((bf16[64,32,128]{2,1,0:T(8,128)(2,1)}), bf16[64,32,128]{2,1,0:T(8,128)(2,1)S(1)}, u32[]{:S(2)}, u32[]{:S(2)}) async-start(bf16[64,32,128]{2,1,0:T(8,128)(2,1)} %stack.8), calls=%async_computation | async-start | bytes 1048576 | tf_op jit(solution)/shard_map/all_to_all | solution.py:80
  31.9 197.8 %all_gather.6 = bf16[2048,128]{1,0:T(8,128)(2,1)S(1)} all-gather(bf16[32,128]{1,0:T(8,128)(2,1)S(1)} %copy-done.4), channel_id=1, replica_groups=mesh['blk'=64,'mp'=8] {'blk'}, dimensions={0}, use_global_device_ids=true | all-gather | bytes 532480 | tf_op jit(solution)/shard_map/all_gather | solution.py:83
  233.6 2.4 fusion.29
  236.9 311.7 %while.20 = (s32[]{:T(128)}, f32[1,5,256]{2,1,0:T(8,128)S(1)}, f32[1,5,256]{2,1,0:T(8,128)S(1)}, f32[1,5,256,128]{3,2,1,0:T(8,128)S(1)}, bf16[2,256,128]{2,1,0:T...) while((s32[]{:T(128)}, f32[1,5,256]{2,1,0:T(8,128)S(1)}, ...), condition=%wide.region_10.11_spmd.clone, body=%wide.region_6.0_spmd.clone.sunk | while | flops 171328000 | bytes 6847233 | solution.py:106
  236.9 2.2 collective-permute-start
  239.5 15.5 %collective-permute-done = bf16[2,256,128]{2,1,0:T(8,128)(2,1)S(1)} collective-permute-done((bf16[2,256,128]{2,1,0:T(8,128)(2,1)S(1)}, bf16[2,256,128]{2,1,0:T(8,128)(2,1)S(1)}, u32[]{:S(2)}, u32[]{:S(2)}) %collective-permute-start) | collective-permute-done | bytes 131104 | tf_op jit(solution)/shard_map/while/body/eval_jaxpr/ppermute | solution.py:14
  256.2 1.9 collective-permute-start
  258.5 15.8 %collective-permute-done = bf16[2,256,128]{2,1,0:T(8,128)(2,1)S(1)} collective-permute-done((bf16[2,256,128]{2,1,0:T(8,128)(2,1)S(1)}, bf16[2,256,128]{2,1,0:T(8,128)(2,1)S(1)}, u32[]{:S(2)}, u32[]{:S(2)}) %collective-permute-start) | collective-permute-done | bytes 131104 | tf_op jit(solution)/shard_map/while/body/eval_jaxpr/ppermute | solution.py:14
  275.5 1.9 collective-permute-start
  277.8 15.8 %collective-permute-done = bf16[2,256,128]{2,1,0:T(8,128)(2,1)S(1)} collective-permute-done((bf16[2,256,128]{2,1,0:T(8,128)(2,1)S(1)}, bf16[2,256,128]{2,1,0:T(8,128)(2,1)S(1)}, u32[]{:S(2)}, u32[]{:S(2)}) %collective-permute-start) | collective-permute-done | bytes 131104 | tf_op jit(solution)/shard_map/while/body/eval_jaxpr/ppermute | solution.py:14
  294.8 1.9 collective-permute-start
  297.1 18.6 %collective-permute-done = bf16[2,256,128]{2,1,0:T(8,128)(2,1)S(1)} collective-permute-done((bf16[2,256,128]{2,1,0:T(8,128)(2,1)S(1)}, bf16[2,256,128]{2,1,0:T(8,128)(2,1)S(1)}, u32[]{:S(2)}, u32[]{:S(2)}) %collective-permute-start) | collective-permute-done | bytes 131104 | tf_op jit(solution)/shard_map/while/body/eval_jaxpr/ppermute | solution.py:14
  317.0 1.9 collective-permute-start
  319.2 15.8 %collective-permute-done = bf16[2,256,128]{2,1,0:T(8,128)(2,1)S(1)} collective-permute-done((bf16[2,256,128]{2,1,0:T(8,128)(2,1)S(1)}, bf16[2,256,128]{2,1,0:T(8,128)(2,1)S(1)}, u32[]{:S(2)}, u32[]{:S(2)}) %collective-permute-start) | collective-permute-done | bytes 131104 | tf_op jit(solution)/shard_map/while/body/eval_jaxpr/ppermute | solution.py:14
  336.3 1.9 collective-permute-start
  338.5 15.8 %collective-permute-done = bf16[2,256,128]{2,1,0:T(8,128)(2,1)S(1)} collective-permute-done((bf16[2,256,128]{2,1,0:T(8,128)(2,1)S(1)}, bf16[2,256,128]{2,1,0:T(8,128)(2,1)S(1)}, u32[]{:S(2)}, u32[]{:S(2)}) %collective-permute-start) | collective-permute-done | bytes 131104 | tf_op jit(solution)/shard_map/while/body/eval_jaxpr/ppermute | solution.py:14
  357.8 15.8 %collective-permute-done = bf16[2,256,128]{2,1,0:T(8,128)(2,1)S(1)} collective-permute-done((bf16[2,256,128]{2,1,0:T(8,128)(2,1)S(1)}, bf16[2,256,128]{2,1,0:T(8,128)(2,1)S(1)}, u32[]{:S(2)}, u32[]{:S(2)}) %collective-permute-start) | collective-permute-done | bytes 131104 | tf_op jit(solution)/shard_map/while/body/eval_jaxpr/ppermute | solution.py:14
  374.9 1.9 collective-permute-start
  377.1 15.9 %collective-permute-done = bf16[2,256,128]{2,1,0:T(8,128)(2,1)S(1)} collective-permute-done((bf16[2,256,128]{2,1,0:T(8,128)(2,1)S(1)}, bf16[2,256,128]{2,1,0:T(8,128)(2,1)S(1)}, u32[]{:S(2)}, u32[]{:S(2)}) %collective-permute-start) | collective-permute-done | bytes 131104 | tf_op jit(solution)/shard_map/while/body/eval_jaxpr/ppermute | solution.py:14
  396.5 15.8 %collective-permute-done = bf16[2,256,128]{2,1,0:T(8,128)(2,1)S(1)} collective-permute-done((bf16[2,256,128]{2,1,0:T(8,128)(2,1)S(1)}, bf16[2,256,128]{2,1,0:T(8,128)(2,1)S(1)}, u32[]{:S(2)}, u32[]{:S(2)}) %collective-permute-start) | collective-permute-done | bytes 131104 | tf_op jit(solution)/shard_map/while/body/eval_jaxpr/ppermute | solution.py:14
  413.6 1.9 collective-permute-start
  415.8 15.8 %collective-permute-done = bf16[2,256,128]{2,1,0:T(8,128)(2,1)S(1)} collective-permute-done((bf16[2,256,128]{2,1,0:T(8,128)(2,1)S(1)}, bf16[2,256,128]{2,1,0:T(8,128)(2,1)S(1)}, u32[]{:S(2)}, u32[]{:S(2)}) %collective-permute-start) | collective-permute-done | bytes 131104 | tf_op jit(solution)/shard_map/while/body/eval_jaxpr/ppermute | solution.py:14
  435.1 15.8 %collective-permute-done = bf16[2,256,128]{2,1,0:T(8,128)(2,1)S(1)} collective-permute-done((bf16[2,256,128]{2,1,0:T(8,128)(2,1)S(1)}, bf16[2,256,128]{2,1,0:T(8,128)(2,1)S(1)}, u32[]{:S(2)}, u32[]{:S(2)}) %collective-permute-start) | collective-permute-done | bytes 131104 | tf_op jit(solution)/shard_map/while/body/eval_jaxpr/ppermute | solution.py:14
  454.4 15.8 %collective-permute-done = bf16[2,256,128]{2,1,0:T(8,128)(2,1)S(1)} collective-permute-done((bf16[2,256,128]{2,1,0:T(8,128)(2,1)S(1)}, bf16[2,256,128]{2,1,0:T(8,128)(2,1)S(1)}, u32[]{:S(2)}, u32[]{:S(2)}) %collective-permute-start) | collective-permute-done | bytes 131104 | tf_op jit(solution)/shard_map/while/body/eval_jaxpr/ppermute | solution.py:14
  473.7 15.8 %collective-permute-done = bf16[2,256,128]{2,1,0:T(8,128)(2,1)S(1)} collective-permute-done((bf16[2,256,128]{2,1,0:T(8,128)(2,1)S(1)}, bf16[2,256,128]{2,1,0:T(8,128)(2,1)S(1)}, u32[]{:S(2)}, u32[]{:S(2)}) %collective-permute-start) | collective-permute-done | bytes 131104 | tf_op jit(solution)/shard_map/while/body/eval_jaxpr/ppermute | solution.py:14
  493.0 15.8 %collective-permute-done = bf16[2,256,128]{2,1,0:T(8,128)(2,1)S(1)} collective-permute-done((bf16[2,256,128]{2,1,0:T(8,128)(2,1)S(1)}, bf16[2,256,128]{2,1,0:T(8,128)(2,1)S(1)}, u32[]{:S(2)}, u32[]{:S(2)}) %collective-permute-start) | collective-permute-done | bytes 131104 | tf_op jit(solution)/shard_map/while/body/eval_jaxpr/ppermute | solution.py:14
  510.1 1.9 collective-permute-start
  512.3 15.8 %collective-permute-done = bf16[2,256,128]{2,1,0:T(8,128)(2,1)S(1)} collective-permute-done((bf16[2,256,128]{2,1,0:T(8,128)(2,1)S(1)}, bf16[2,256,128]{2,1,0:T(8,128)(2,1)S(1)}, u32[]{:S(2)}, u32[]{:S(2)}) %collective-permute-start) | collective-permute-done | bytes 131104 | tf_op jit(solution)/shard_map/while/body/eval_jaxpr/ppermute | solution.py:14
  531.6 15.8 %collective-permute-done = bf16[2,256,128]{2,1,0:T(8,128)(2,1)S(1)} collective-permute-done((bf16[2,256,128]{2,1,0:T(8,128)(2,1)S(1)}, bf16[2,256,128]{2,1,0:T(8,128)(2,1)S(1)}, u32[]{:S(2)}, u32[]{:S(2)}) %collective-permute-start) | collective-permute-done | bytes 131104 | tf_op jit(solution)/shard_map/while/body/eval_jaxpr/ppermute | solution.py:14
  549.0 5.1 convolution_convert_fusion
  554.1 2.6 copy.49
  556.7 65.1 %reduce-scatter.4.cloned.1.call-done = bf16[640,256]{1,0:T(8,128)(2,1)} async-done(((bf16[5120,256]{1,0:T(8,128)(2,1)}), bf16[640,256]{1,0:T(8,128)(2,1)}) %reduce-scatter.4.cloned.1.call-update) | async-done | bytes 327696
  (222 shorter events, 48.4 us)
Async XLA Ops:
  6.5 23.7 %copy-start = (bf16[256,640]{1,0:T(8,128)(2,1)S(1)}, bf16[256,640]{1,0:T(8,128)(2,1)}, u32[]{:S(2)}) copy-start(bf16[256,640]{1,0:T(8,128)(2,1)} %param.9) | copy-start | bytes 983044
  6.5 23.9 %copy-start.5 = (s32[16]{0:T(128)S(1)}, s32[16]{0:T(128)}, u32[]{:S(2)}) copy-start(s32[16]{0:T(128)} %param.15) | copy-start | bytes 196
  8.2 22.9 %copy-start.1 = (bf16[256,128]{1,0:T(8,128)(2,1)S(1)}, bf16[256,128]{1,0:T(8,128)(2,1)}, u32[]{:S(2)}) copy-start(bf16[256,128]{1,0:T(8,128)(2,1)} %param.10) | copy-start | bytes 196612
  8.2 22.9 %copy-start.2 = (bf16[256,128]{1,0:T(8,128)(2,1)S(1)}, bf16[256,128]{1,0:T(8,128)(2,1)}, u32[]{:S(2)}) copy-start(bf16[256,128]{1,0:T(8,128)(2,1)} %param.11) | copy-start | bytes 196612
  8.2 23.7 %copy-start.4 = (bf16[32,128]{1,0:T(8,128)(2,1)S(1)}, bf16[32,128]{1,0:T(8,128)(2,1)}, u32[]{:S(2)}) copy-start(bf16[32,128]{1,0:T(8,128)(2,1)} %param.13) | copy-start | bytes 24580
  8.2 222.0 %all-to-all-start = ((bf16[64,32,128]{2,1,0:T(8,128)(2,1)}), bf16[64,32,128]{2,1,0:T(8,128)(2,1)S(1)}, u32[]{:S(2)}, u32[]{:S(2)}) async-start(bf16[64,32,128]{2,1,0:T(8,128)(2,1)} %stack.8), calls=%async_computation | async-start | bytes 1048576 | tf_op jit(solution)/shard_map/all_to_all | solution.py:80
  29.5 519.5 %all-gather.2.cloned.1.call-start = ((), (), s32[]{:S(2)}) async-start(), calls=%async_computation.2 | async-start | bytes 6656000 | tf_op jit(solution)/shard_map/all_gather | solution.py:116
  30.2 591.6 %reduce-scatter.4.cloned.1.call-start = ((), (), s32[]{:S(2)}) async-start(), calls=%async_computation.3 | async-start | bytes 2949120
  236.0 0.9 copy-start.3
  236.9 18.0 %collective-permute-start = (bf16[2,256,128]{2,1,0:T(8,128)(2,1)S(1)}, bf16[2,256,128]{2,1,0:T(8,128)(2,1)S(1)}, u32[]{:S(2)}, u32[]{:S(2)}) collective-permute-start(bf16[2,256,128]{2,1,0:T(8,128)(2,1)S(1)} %get-tuple-element.371), channel_id=1, source_target_pairs={{0,8},{8,16},{16,24},{24,32},{32,40},{40,48},{48,56},{56,64},{64,7... | collective-permute-start | bytes 393224 | tf_op jit(solution)/shard_map/while/body/eval_jaxpr/ppermute | solution.py:14
  256.2 18.0 %collective-permute-start = (bf16[2,256,128]{2,1,0:T(8,128)(2,1)S(1)}, bf16[2,256,128]{2,1,0:T(8,128)(2,1)S(1)}, u32[]{:S(2)}, u32[]{:S(2)}) collective-permute-start(bf16[2,256,128]{2,1,0:T(8,128)(2,1)S(1)} %get-tuple-element.371), channel_id=1, source_target_pairs={{0,8},{8,16},{16,24},{24,32},{32,40},{40,48},{48,56},{56,64},{64,7... | collective-permute-start | bytes 393224 | tf_op jit(solution)/shard_map/while/body/eval_jaxpr/ppermute | solution.py:14
  275.5 18.0 %collective-permute-start = (bf16[2,256,128]{2,1,0:T(8,128)(2,1)S(1)}, bf16[2,256,128]{2,1,0:T(8,128)(2,1)S(1)}, u32[]{:S(2)}, u32[]{:S(2)}) collective-permute-start(bf16[2,256,128]{2,1,0:T(8,128)(2,1)S(1)} %get-tuple-element.371), channel_id=1, source_target_pairs={{0,8},{8,16},{16,24},{24,32},{32,40},{40,48},{48,56},{56,64},{64,7... | collective-permute-start | bytes 393224 | tf_op jit(solution)/shard_map/while/body/eval_jaxpr/ppermute | solution.py:14
  294.8 20.8 %collective-permute-start = (bf16[2,256,128]{2,1,0:T(8,128)(2,1)S(1)}, bf16[2,256,128]{2,1,0:T(8,128)(2,1)S(1)}, u32[]{:S(2)}, u32[]{:S(2)}) collective-permute-start(bf16[2,256,128]{2,1,0:T(8,128)(2,1)S(1)} %get-tuple-element.371), channel_id=1, source_target_pairs={{0,8},{8,16},{16,24},{24,32},{32,40},{40,48},{48,56},{56,64},{64,7... | collective-permute-start | bytes 393224 | tf_op jit(solution)/shard_map/while/body/eval_jaxpr/ppermute | solution.py:14
  317.0 18.0 %collective-permute-start = (bf16[2,256,128]{2,1,0:T(8,128)(2,1)S(1)}, bf16[2,256,128]{2,1,0:T(8,128)(2,1)S(1)}, u32[]{:S(2)}, u32[]{:S(2)}) collective-permute-start(bf16[2,256,128]{2,1,0:T(8,128)(2,1)S(1)} %get-tuple-element.371), channel_id=1, source_target_pairs={{0,8},{8,16},{16,24},{24,32},{32,40},{40,48},{48,56},{56,64},{64,7... | collective-permute-start | bytes 393224 | tf_op jit(solution)/shard_map/while/body/eval_jaxpr/ppermute | solution.py:14
  336.3 18.0 %collective-permute-start = (bf16[2,256,128]{2,1,0:T(8,128)(2,1)S(1)}, bf16[2,256,128]{2,1,0:T(8,128)(2,1)S(1)}, u32[]{:S(2)}, u32[]{:S(2)}) collective-permute-start(bf16[2,256,128]{2,1,0:T(8,128)(2,1)S(1)} %get-tuple-element.371), channel_id=1, source_target_pairs={{0,8},{8,16},{16,24},{24,32},{32,40},{40,48},{48,56},{56,64},{64,7... | collective-permute-start | bytes 393224 | tf_op jit(solution)/shard_map/while/body/eval_jaxpr/ppermute | solution.py:14
  355.6 18.0 %collective-permute-start = (bf16[2,256,128]{2,1,0:T(8,128)(2,1)S(1)}, bf16[2,256,128]{2,1,0:T(8,128)(2,1)S(1)}, u32[]{:S(2)}, u32[]{:S(2)}) collective-permute-start(bf16[2,256,128]{2,1,0:T(8,128)(2,1)S(1)} %get-tuple-element.371), channel_id=1, source_target_pairs={{0,8},{8,16},{16,24},{24,32},{32,40},{40,48},{48,56},{56,64},{64,7... | collective-permute-start | bytes 393224 | tf_op jit(solution)/shard_map/while/body/eval_jaxpr/ppermute | solution.py:14
  374.9 18.1 %collective-permute-start = (bf16[2,256,128]{2,1,0:T(8,128)(2,1)S(1)}, bf16[2,256,128]{2,1,0:T(8,128)(2,1)S(1)}, u32[]{:S(2)}, u32[]{:S(2)}) collective-permute-start(bf16[2,256,128]{2,1,0:T(8,128)(2,1)S(1)} %get-tuple-element.371), channel_id=1, source_target_pairs={{0,8},{8,16},{16,24},{24,32},{32,40},{40,48},{48,56},{56,64},{64,7... | collective-permute-start | bytes 393224 | tf_op jit(solution)/shard_map/while/body/eval_jaxpr/ppermute | solution.py:14
  394.3 18.0 %collective-permute-start = (bf16[2,256,128]{2,1,0:T(8,128)(2,1)S(1)}, bf16[2,256,128]{2,1,0:T(8,128)(2,1)S(1)}, u32[]{:S(2)}, u32[]{:S(2)}) collective-permute-start(bf16[2,256,128]{2,1,0:T(8,128)(2,1)S(1)} %get-tuple-element.371), channel_id=1, source_target_pairs={{0,8},{8,16},{16,24},{24,32},{32,40},{40,48},{48,56},{56,64},{64,7... | collective-permute-start | bytes 393224 | tf_op jit(solution)/shard_map/while/body/eval_jaxpr/ppermute | solution.py:14
  413.6 18.0 %collective-permute-start = (bf16[2,256,128]{2,1,0:T(8,128)(2,1)S(1)}, bf16[2,256,128]{2,1,0:T(8,128)(2,1)S(1)}, u32[]{:S(2)}, u32[]{:S(2)}) collective-permute-start(bf16[2,256,128]{2,1,0:T(8,128)(2,1)S(1)} %get-tuple-element.371), channel_id=1, source_target_pairs={{0,8},{8,16},{16,24},{24,32},{32,40},{40,48},{48,56},{56,64},{64,7... | collective-permute-start | bytes 393224 | tf_op jit(solution)/shard_map/while/body/eval_jaxpr/ppermute | solution.py:14
  432.9 18.0 %collective-permute-start = (bf16[2,256,128]{2,1,0:T(8,128)(2,1)S(1)}, bf16[2,256,128]{2,1,0:T(8,128)(2,1)S(1)}, u32[]{:S(2)}, u32[]{:S(2)}) collective-permute-start(bf16[2,256,128]{2,1,0:T(8,128)(2,1)S(1)} %get-tuple-element.371), channel_id=1, source_target_pairs={{0,8},{8,16},{16,24},{24,32},{32,40},{40,48},{48,56},{56,64},{64,7... | collective-permute-start | bytes 393224 | tf_op jit(solution)/shard_map/while/body/eval_jaxpr/ppermute | solution.py:14
  452.2 18.0 %collective-permute-start = (bf16[2,256,128]{2,1,0:T(8,128)(2,1)S(1)}, bf16[2,256,128]{2,1,0:T(8,128)(2,1)S(1)}, u32[]{:S(2)}, u32[]{:S(2)}) collective-permute-start(bf16[2,256,128]{2,1,0:T(8,128)(2,1)S(1)} %get-tuple-element.371), channel_id=1, source_target_pairs={{0,8},{8,16},{16,24},{24,32},{32,40},{40,48},{48,56},{56,64},{64,7... | collective-permute-start | bytes 393224 | tf_op jit(solution)/shard_map/while/body/eval_jaxpr/ppermute | solution.py:14
  471.5 18.0 %collective-permute-start = (bf16[2,256,128]{2,1,0:T(8,128)(2,1)S(1)}, bf16[2,256,128]{2,1,0:T(8,128)(2,1)S(1)}, u32[]{:S(2)}, u32[]{:S(2)}) collective-permute-start(bf16[2,256,128]{2,1,0:T(8,128)(2,1)S(1)} %get-tuple-element.371), channel_id=1, source_target_pairs={{0,8},{8,16},{16,24},{24,32},{32,40},{40,48},{48,56},{56,64},{64,7... | collective-permute-start | bytes 393224 | tf_op jit(solution)/shard_map/while/body/eval_jaxpr/ppermute | solution.py:14
  490.8 18.0 %collective-permute-start = (bf16[2,256,128]{2,1,0:T(8,128)(2,1)S(1)}, bf16[2,256,128]{2,1,0:T(8,128)(2,1)S(1)}, u32[]{:S(2)}, u32[]{:S(2)}) collective-permute-start(bf16[2,256,128]{2,1,0:T(8,128)(2,1)S(1)} %get-tuple-element.371), channel_id=1, source_target_pairs={{0,8},{8,16},{16,24},{24,32},{32,40},{40,48},{48,56},{56,64},{64,7... | collective-permute-start | bytes 393224 | tf_op jit(solution)/shard_map/while/body/eval_jaxpr/ppermute | solution.py:14
  510.1 18.0 %collective-permute-start = (bf16[2,256,128]{2,1,0:T(8,128)(2,1)S(1)}, bf16[2,256,128]{2,1,0:T(8,128)(2,1)S(1)}, u32[]{:S(2)}, u32[]{:S(2)}) collective-permute-start(bf16[2,256,128]{2,1,0:T(8,128)(2,1)S(1)} %get-tuple-element.371), channel_id=1, source_target_pairs={{0,8},{8,16},{16,24},{24,32},{32,40},{40,48},{48,56},{56,64},{64,7... | collective-permute-start | bytes 393224 | tf_op jit(solution)/shard_map/while/body/eval_jaxpr/ppermute | solution.py:14
  529.4 18.0 %collective-permute-start = (bf16[2,256,128]{2,1,0:T(8,128)(2,1)S(1)}, bf16[2,256,128]{2,1,0:T(8,128)(2,1)S(1)}, u32[]{:S(2)}, u32[]{:S(2)}) collective-permute-start(bf16[2,256,128]{2,1,0:T(8,128)(2,1)S(1)} %get-tuple-element.371), channel_id=1, source_target_pairs={{0,8},{8,16},{16,24},{24,32},{32,40},{40,48},{48,56},{56,64},{64,7... | collective-permute-start | bytes 393224 | tf_op jit(solution)/shard_map/while/body/eval_jaxpr/ppermute | solution.py:14
Sparse Core Ops, SparseCore 0:
  34.8 166.9 all-gather.1
  556.8 64.9 reduce-scatter.3
